TPU v7x, 512 devices: a whole 4x8x8 slice. The times are simulated.
512 devices in a mesh: row: 4 (over y_hi), col: 16 (over y_lo, x, core), depth: 8 (over z).
Axes of the slice: x: 4, y: 8 (y_hi: 4, y_lo: 2; y = y_hi * 2 + y_lo), z: 8, core: 2. Of those that a mesh axis runs over, the one named last changes fastest.
Arguments:
- block_values: bfloat16 [32, 16, 16, 128, 128], P(('row', 'depth'), 'col'), may hold values from 0.0049743652 to 0.5
- block_cols: int32 [32, 16, 16], P(('row', 'depth'), 'col'), may hold values from 0 to 511, as said below
- live_count: int32 [32, 16], P(('row', 'depth'), 'col'), may hold values from 8 to 16, as said below
- out_pattern: int32 [4, 16, 32, 2], P('row', 'col'), may hold values from 0 to 511, as said below
Outputs:
- squared_log: bfloat16 [4, 16, 32, 128, 128], P('row', 'col', 'depth')
Inputs may be any that keep to these rules, and one draw needn't show every extreme that they name: Block row i's blocks are its first live_count slots; in every draw some block row is full. `block_cols`: the slots of one block row name distinct block columns. Call (k // 16) % 8 the depth part of a block index k and k // 32 its column group. Among the live slots of one block row at most 2 name a column in any one depth part and at most 2 in any one column group; both bounds are reached in every draw. The 32 entries of out_pattern[r, c] are distinct pairs (i, j) with i // 128 == r and j // 32 == c.
All inputs are finite; a program needn't handle non-finite values.
Results may differ from a plain program's by a relative error of at most 0.001.
Values may be sent and summed in bfloat16 or wider, within the bound.
No kernel may reach another device: no remote copies, remote signals or barrier semaphores. Data moves between devices by JAX's collectives and lax.ppermute only.
A program may use at most 128 MiB of HBM per device.

v0:
```python
import math
import jax
import jax.numpy as jnp
from jax import lax
from jax.sharding import PartitionSpec as P


def pack_slots(values, col_ids, targets, is_live, part_count, capacity):
    row_count = col_ids.shape[0]
    block_size = values.shape[-1]
    chosen = (
        targets[:, :, None] == jnp.arange(part_count, dtype=jnp.int32)[None, None, :]
    ) & is_live[:, :, None]
    running = jnp.cumsum(chosen.astype(jnp.int32), axis=1) - 1
    order_in = jnp.sum(jnp.where(chosen, running, 0), axis=2)
    row_ids = jnp.arange(row_count, dtype=jnp.int32)[:, None]
    total = part_count * row_count * capacity
    position = (targets * row_count + row_ids) * capacity + order_in
    position = jnp.where(is_live, position, total).reshape(-1)
    packed = jnp.zeros((total, block_size, block_size), values.dtype)
    packed = packed.at[position].set(values.reshape(-1, block_size, block_size), mode="drop")
    packed_cols = (
        jnp.full((total,), -1, jnp.int32).at[position].set(col_ids.reshape(-1), mode="drop")
    )
    return (
        packed.reshape(part_count, row_count, capacity, block_size, block_size),
        packed_cols.reshape(part_count, row_count, capacity),
    )


def gather_by_exchange(x, axis, size):
    copies = jnp.broadcast_to(x[None], (size,) + x.shape)
    return lax.all_to_all(copies, axis, split_axis=0, concat_axis=0, tiled=True)


def body(block_values, block_cols, live_count, out_pattern):
    depths = lax.axis_size("depth")
    columns = lax.axis_size("col")
    row_groups = lax.axis_size("row")
    row_index = lax.axis_index("row")
    rows_dev = block_values.shape[1]
    slot_count = block_values.shape[2]
    block_size = block_values.shape[3]
    group_rows = columns * rows_dev
    group_count = row_groups * depths
    total_rows = group_count * group_rows
    col_block = total_rows // columns
    pair_size = group_count // columns
    cap_left = slot_count // depths
    cap_right = pair_size * (slot_count // group_count) + min(pair_size, slot_count % group_count)
    values = block_values.reshape(rows_dev, slot_count, block_size, block_size)
    col_ids = block_cols.reshape(rows_dev, slot_count)
    counts = live_count.reshape(rows_dev)
    is_live = jnp.arange(slot_count, dtype=jnp.int32)[None, :] < counts[:, None]
    left_vals, left_cols = pack_slots(
        values, col_ids, col_ids // group_rows % depths, is_live, depths, cap_left
    )
    left_vals, left_cols = (
        lax.all_to_all(left_vals, "depth", split_axis=0, concat_axis=0, tiled=True),
        lax.all_to_all(left_cols, "depth", split_axis=0, concat_axis=0, tiled=True),
    )
    left_vals, left_cols = (
        lax.all_gather(left_vals[None], "col", axis=0, tiled=True),
        gather_by_exchange(left_cols, "col", columns),
    )
    left_shape = left_cols.shape
    source_col = lax.broadcasted_iota(jnp.int32, left_shape, 0)
    source_depth = lax.broadcasted_iota(jnp.int32, left_shape, 1)
    source_row = lax.broadcasted_iota(jnp.int32, left_shape, 2)
    left_rows = (
        (row_index * depths + source_depth) * group_rows + source_col * rows_dev + source_row
    ).reshape(-1)
    left_flat = left_vals.reshape(-1, block_size, block_size)
    left_ids = left_cols.reshape(-1)
    right_vals, right_cols = pack_slots(
        values, col_ids, col_ids // col_block, is_live, columns, cap_right
    )
    right_vals, right_cols = (
        lax.all_to_all(right_vals, "col", split_axis=0, concat_axis=0, tiled=True),
        lax.all_to_all(right_cols, "col", split_axis=0, concat_axis=0, tiled=True),
    )
    right_vals, right_cols = (
        lax.all_gather(right_vals[None], "row", axis=0, tiled=True),
        gather_by_exchange(right_cols, "row", row_groups),
    )
    right_flat = right_vals.reshape(-1, cap_right, block_size, block_size)
    right_ids = right_cols.reshape(-1, cap_right)
    pattern_rows = out_pattern[0, 0, :, 0]
    pattern_cols = out_pattern[0, 0, :, 1]
    local_row = pattern_rows - row_index * (depths * group_rows)
    left_pos = local_row % group_rows * depths + local_row // group_rows
    left_sel = left_pos[:, None] * cap_left + jnp.arange(cap_left, dtype=jnp.int32)[None, :]
    left_flat = left_vals.reshape(-1, block_size, block_size)
    left_ids = left_cols.reshape(-1)
    left_pick = jnp.take(left_flat, left_sel.reshape(-1), axis=0)
    inner = jnp.take(left_ids, left_sel, axis=0)
    safe_inner = jnp.maximum(inner, 0)
    right_row = safe_inner // (depths * group_rows) * columns + safe_inner % group_rows
    right_ids = right_cols.reshape(-1, cap_right)
    right_flat = right_vals.reshape(-1, block_size, block_size)
    right_here = jnp.take(right_ids, right_row, axis=0)
    matched = (right_here == pattern_cols[:, None, None]) & (inner >= 0)[:, :, None]
    slot = jnp.sum(
        jnp.where(matched, jnp.arange(cap_right, dtype=jnp.int32)[None, None, :], 0), axis=2
    )
    found = jnp.any(matched, axis=2)
    right_pick = jnp.take(right_flat, (right_row * cap_right + slot).reshape(-1), axis=0)
    right_pick = jnp.where(found.reshape(-1)[:, None, None], right_pick, jnp.zeros_like(right_pick))
    pattern_len = pattern_rows.shape[0]
    left_pick = left_pick.reshape(pattern_len, cap_left, block_size, block_size)
    right_pick = right_pick.reshape(pattern_len, cap_left, block_size, block_size)
    partial_sum = jnp.einsum(
        "pqab,pqbc->pac", left_pick, right_pick, preferred_element_type=jnp.float32
    )
    share = lax.psum_scatter(partial_sum[None, None], "depth", scatter_dimension=2, tiled=True)
    return jnp.log1p(share).astype(jnp.bfloat16)


def solution(mesh):
    in_specs = (
        P(("row", "depth"), "col", None, None, None),
        P(("row", "depth"), "col", None),
        P(("row", "depth"), "col"),
        P("row", "col", None, None),
    )
    out_specs = P("row", "col", "depth", None, None)
    return jax.shard_map(body, mesh=mesh, in_specs=in_specs, out_specs=out_specs, check_vma=False)
```

profile of v0, /device:TPU:4, one launch (start us, length us, event | category | flops | bytes accessed | tf_op | source)
XLA Modules:
  0.0 247.1 jit_solution(16107756363442089522)
XLA Ops:
  7.2 0.7 and_select_fusion.7
  8.3 0.2 select_reduce_fusion.1
  8.5 0.7 fusion.30
  9.2 0.2 broadcast_in_dim.137
  9.4 2.1 scatter_fusion.1
  11.5 21.9 %all_to_all.30 = bf16[16,1,2,128,128]{4,3,2,1,0:T(8,128)(2,1)} all-to-all(bf16[16,1,2,128,128]{4,3,2,1,0:T(8,128)(2,1)S(1)} %bitcast.96), channel_id=1, replica_groups=mesh['row'=4,'col'=16,'depth'=8] {'col'}, dimensions={0} | all-to-all | bytes 2097152 | tf_op jit(solution)/shard_map/all_to_all | solution.py:79
  33.6 1.1 scatter_fusion
  34.8 25.3 %all_to_all.31 = bf16[8,1,2,128,128]{4,3,2,1,0:T(8,128)(2,1)} all-to-all(bf16[8,1,2,128,128]{4,3,2,1,0:T(8,128)(2,1)S(1)} %bitcast.97), channel_id=1, replica_groups=mesh['row'=4,'col'=16,'depth'=8] {'depth'}, dimensions={0} | all-to-all | bytes 1048576 | tf_op jit(solution)/shard_map/all_to_all | solution.py:59
  60.1 0.8 scatter_custom_fusion.2
  60.9 0.7 reshape.1075
  61.6 5.9 %all-to-all-start.3 = ((s32[16,1,2]{2,1,0:T(1,128)}), s32[16,1,2]{2,1,0:T(1,128)S(1)}, u32[]{:S(2)}, u32[]{:S(2)}) async-start(s32[16,1,2]{2,1,0:T(1,128)} %bitcast.15), calls=%async_computation.3 | async-start | bytes 16384 | tf_op jit(solution)/shard_map/all_to_all | solution.py:80
  67.5 0.8 scatter_custom_fusion.1
  68.2 0.7 reshape.1073
  68.9 2.3 all-to-all-done.3
  71.2 3.3 %all-to-all-start.1 = ((s32[8,1,2]{2,1,0:T(1,128)}), s32[8,1,2]{2,1,0:T(1,128)S(1)}, u32[]{:S(2)}, u32[]{:S(2)}) async-start(s32[8,1,2]{2,1,0:T(1,128)} %bitcast.11), calls=%async_computation.1 | async-start | bytes 8192 | tf_op jit(solution)/shard_map/all_to_all | solution.py:60
  74.6 7.4 %all-to-all-done.1 = s32[8,1,2]{2,1,0:T(1,128)S(1)} async-done(((s32[8,1,2]{2,1,0:T(1,128)}), s32[8,1,2]{2,1,0:T(1,128)S(1)}, u32[]{:S(2)}, u32[]{:S(2)}) %all-to-all-start.1) | async-done | bytes 96 | tf_op jit(solution)/shard_map/all_to_all | solution.py:60
  82.1 0.6 broadcast_in_dim.130
  82.7 6.2 %all-to-all-start.4 = ((s32[4,16,1,2]{1,3,2,0:T(2,128)}), s32[4,16,1,2]{1,3,2,0:T(2,128)S(1)}, u32[]{:S(2)}, u32[]{:S(2)}) async-start(s32[4,16,1,2]{1,3,2,0:T(2,128)} %broadcast_in_dim.130), calls=%async_computation.4 | async-start | bytes 8192 | tf_op jit(solution)/shard_map/all_to_all | solution.py:33
  89.0 7.5 %all-to-all-done.4 = s32[4,16,1,2]{1,3,2,0:T(2,128)S(1)} async-done(((s32[4,16,1,2]{1,3,2,0:T(2,128)}), s32[4,16,1,2]{1,3,2,0:T(2,128)S(1)}, u32[]{:S(2)}, u32[]{:S(2)}) %all-to-all-start.4) | async-done | bytes 544 | tf_op jit(solution)/shard_map/all_to_all | solution.py:33
  96.6 0.6 broadcast_in_dim.125
  97.2 6.9 %all-to-all-start.2 = ((s32[16,8,1,2]{1,3,2,0:T(2,128)}), s32[16,8,1,2]{1,3,2,0:T(2,128)S(1)}, u32[]{:S(2)}, u32[]{:S(2)}) async-start(s32[16,8,1,2]{1,3,2,0:T(2,128)} %broadcast_in_dim.125), calls=%async_computation.2 | async-start | bytes 32768 | tf_op jit(solution)/shard_map/all_to_all | solution.py:33
  104.7 3.6 %all-to-all-done.2 = s32[16,8,1,2]{1,3,2,0:T(2,128)S(1)} async-done(((s32[16,8,1,2]{1,3,2,0:T(2,128)}), s32[16,8,1,2]{1,3,2,0:T(2,128)S(1)}, u32[]{:S(2)}, u32[]{:S(2)}) %all-to-all-start.2) | async-done | bytes 1056 | tf_op jit(solution)/shard_map/all_to_all | solution.py:33
  108.6 0.8 gather_fusion.1
  109.8 0.6 gather_fusion.2
  110.4 0.3 copy.55
  111.6 12.6 %all-gather.7.cloned.1.call-done = bf16[64,1,2,128,128]{4,3,2,1,0:T(8,128)(2,1)} async-done(((bf16[16,1,2,128,128]{4,3,2,1,0:T(8,128)(2,1)}), bf16[64,1,2,128,128]{4,3,2,1,0:T(8,128)(2,1)}) %all-gather.7.cloned.1.call-update) | async-done | bytes 4194320 | tf_op jit(solution)/shard_map/all_gather | solution.py:83
  124.2 3.1 %gather_fusion.3 = bf16[64,128,128]{2,1,0:T(8,128)(2,1)S(1)} fusion(bf16[128,128,128]{2,1,0:T(8,128)(2,1)} %bitcast.103, s32[1024]{0:T(1024)S(1)} %pad_clamp_fusion), kind=kCustom, calls=%fused_computation.3 | custom fusion | bytes 4194560 | tf_op jit(solution)/shard_map/jit(_take)/gather | solution.py:107
  127.3 55.0 %all-gather.5.cloned.1.call-done = bf16[128,1,2,128,128]{4,3,2,1,0:T(8,128)(2,1)} async-done(((bf16[8,1,2,128,128]{4,3,2,1,0:T(8,128)(2,1)}), bf16[128,1,2,128,128]{4,3,2,1,0:T(8,128)(2,1)}) %all-gather.5.cloned.1.call-update) | async-done | bytes 8388624 | tf_op jit(solution)/shard_map/all_gather | solution.py:63
  182.3 5.6 %gather_fusion = bf16[64,128,128]{2,1,0:T(8,128)(2,1)} fusion(bf16[256,128,128]{2,1,0:T(8,128)(2,1)} %bitcast.104, s32[1024]{0:T(1024)S(1)} %pad_clamp_fusion.3), kind=kCustom, calls=%fused_computation | custom fusion | bytes 4194560 | tf_op jit(solution)/shard_map/jit(_take)/gather | solution.py:95
  187.9 3.7 %fusion.7 = f32[1,1,32,128,128]{4,3,2,1,0:T(8,128)} fusion(bf16[32,2,128,128]{3,2,1,0:T(8,128)(2,1)S(1)} %bitcast.99, pred[32,2]{1,0:T(8,128)(4,1)S(1)} %copy.52, pred[32,2]{1,0:T(8,128)(4,1)S(1)} %get-tuple-element.5, bf16[32,2,128,128]{3,2,1,0:T(8,128)(2,1)} %bitcast.100, pred[32,2]{1,0:T(8,128)(4,1)S(1)} %copy.38), kind=kOutput, calls=%fused_computation.15 | convolution fusion | flops 271581184 | bytes 6291648 | tf_op jit(solution)/shard_map/pqab,pqbc->pac/dot_general | solution.py:112
  191.6 47.2 %reduce-scatter.2.cloned.1.call-done = f32[1,1,4,128,128]{4,3,2,1,0:T(8,128)} async-done(((f32[1,1,32,128,128]{4,3,2,1,0:T(8,128)}), f32[1,1,4,128,128]{4,3,2,1,0:T(8,128)}) %reduce-scatter.2.cloned.1.call-update) | async-done | bytes 262160 | tf_op jit(solution)/shard_map/reduce_scatter | solution.py:115
  238.9 1.7 log-plus-one_convert_fusion
  (52 shorter events, 3.0 us)
Async XLA Ops:
  6.5 117.7 %all-gather.7.cloned.1.call-start = ((), (), s32[]{:S(2)}) async-start(), calls=%async_computation.9 | async-start | bytes 5242880 | tf_op jit(solution)/shard_map/all_gather | solution.py:83
  11.5 22.1 %copy-start = (bf16[1,1,16,128,128]{4,3,2,1,0:T(8,128)(2,1)S(1)}, bf16[1,1,16,128,128]{4,3,2,1,0:T(8,128)(2,1)}, u32[]{:S(2)}) copy-start(bf16[1,1,16,128,128]{4,3,2,1,0:T(8,128)(2,1)} %param.4) | copy-start | bytes 1572868
  33.5 34.0 %copy-start.1 = (s32[1,1,32,2]{2,3,1,0:T(2,128)S(1)}, s32[1,1,32,2]{2,3,1,0:T(2,128)}, u32[]{:S(2)}) copy-start(s32[1,1,32,2]{2,3,1,0:T(2,128)} %param.7) | copy-start | bytes 772
  33.5 148.8 %all-gather.5.cloned.1.call-start = ((), (), s32[]{:S(2)}) async-start(), calls=%async_computation.8 | async-start | bytes 8912896 | tf_op jit(solution)/shard_map/all_gather | solution.py:63
  61.6 9.6 %all-to-all-start.3 = ((s32[16,1,2]{2,1,0:T(1,128)}), s32[16,1,2]{2,1,0:T(1,128)S(1)}, u32[]{:S(2)}, u32[]{:S(2)}) async-start(s32[16,1,2]{2,1,0:T(1,128)} %bitcast.15), calls=%async_computation.3 | async-start | bytes 16384 | tf_op jit(solution)/shard_map/all_to_all | solution.py:80
  71.2 10.9 %all-to-all-start.1 = ((s32[8,1,2]{2,1,0:T(1,128)}), s32[8,1,2]{2,1,0:T(1,128)S(1)}, u32[]{:S(2)}, u32[]{:S(2)}) async-start(s32[8,1,2]{2,1,0:T(1,128)} %bitcast.11), calls=%async_computation.1 | async-start | bytes 8192 | tf_op jit(solution)/shard_map/all_to_all | solution.py:60
  82.7 13.9 %all-to-all-start.4 = ((s32[4,16,1,2]{1,3,2,0:T(2,128)}), s32[4,16,1,2]{1,3,2,0:T(2,128)S(1)}, u32[]{:S(2)}, u32[]{:S(2)}) async-start(s32[4,16,1,2]{1,3,2,0:T(2,128)} %broadcast_in_dim.130), calls=%async_computation.4 | async-start | bytes 8192 | tf_op jit(solution)/shard_map/all_to_all | solution.py:33
  97.2 11.1 %all-to-all-start.2 = ((s32[16,8,1,2]{1,3,2,0:T(2,128)}), s32[16,8,1,2]{1,3,2,0:T(2,128)S(1)}, u32[]{:S(2)}, u32[]{:S(2)}) async-start(s32[16,8,1,2]{1,3,2,0:T(2,128)} %broadcast_in_dim.125), calls=%async_computation.2 | async-start | bytes 32768 | tf_op jit(solution)/shard_map/all_to_all | solution.py:33
  104.1 134.8 %reduce-scatter.2.cloned.1.call-start = ((), (), s32[]{:S(2)}) async-start(), calls=%async_computation.7 | async-start | bytes 2359296 | tf_op jit(solution)/shard_map/reduce_scatter | solution.py:115
Sparse Core Ops, SparseCore 0:
  33.6 90.5 all-gather.6
  126.3 55.9 all-gather.4
  191.8 47.0 reduce-scatter.1
where the time goes:
time: 248 us; the launch traced here: 247 us
  waiting for transfers between devices  136 us (55%)
  blocking collectives  47.3 us (19%)
  starting transfers between devices  22.4 us (9%)
  local copies, waits for them, and re-layouts  20.1 us (8%)
  between operations  14 us (6%)
  other arithmetic  4 us (2%)
  matrix products  3.74 us (2%)
    all_gather x1, waiting for transfers between devices, body(): lax.all_gather(left_vals[None], 'col', axis=0, tiled=True)  55 us
    reduce_scatter x1, waiting for transfers between devices, body(): lax.psum_scatter(partial_sum[None, None], 'depth', scatter_dimension=2, t...  47.2 us
    all_to_all x1, blocking collectives, body(): lax.all_to_all(left_vals, 'depth', split_axis=0, concat_axis=0, tiled=True)  25.3 us
    all_to_all x1, blocking collectives, body(): lax.all_to_all(right_vals, 'col', split_axis=0, concat_axis=0, tiled=True)  21.9 us
    all_to_all x2, starting transfers between devices, gather_by_exchange(): return lax.all_to_all(copies, axis, split_axis=0, concat_axis=0, tiled=True)  13.1 us
    all_gather x1, waiting for transfers between devices, body(): lax.all_gather(right_vals[None], 'row', axis=0, tiled=True)  12.6 us
    all_to_all x2, waiting for transfers between devices, gather_by_exchange(): return lax.all_to_all(copies, axis, split_axis=0, concat_axis=0, tiled=True)  11.2 us
    all_to_all x1, waiting for transfers between devices, body(): lax.all_to_all(left_cols, 'depth', split_axis=0, concat_axis=0, tiled=True)  7.44 us
  transfers between devices with their start and end apart: 7, of which 7 were waited for; matrix products, arithmetic and copies ran while one was open for 5% of the time, Pallas kernels for 0%

commit v1 on v0

--- a/solution.py
+++ b/solution.py
@@ -3,6 +3,11 @@
 import jax.numpy as jnp
 from jax import lax
 from jax.sharding import PartitionSpec as P
+
+
+def gather_over(x, axis, along):
+    repeated = jnp.stack([x] * lax.axis_size(axis))
+    return jnp.concatenate(lax.all_to_all(repeated, axis, 0, 0), axis=along)
 
 
 def pack_slots(values, col_ids, targets, is_live, part_count, capacity):
@@ -60,7 +65,7 @@
         lax.all_to_all(left_cols, "depth", split_axis=0, concat_axis=0, tiled=True),
     )
     left_vals, left_cols = (
-        lax.all_gather(left_vals[None], "col", axis=0, tiled=True),
+        gather_over(left_vals[None], "col", 0),
         gather_by_exchange(left_cols, "col", columns),
     )
     left_shape = left_cols.shape

time: 248 us -> 349 us (1.41)
  waiting for transfers between devices: 136 us -> 241 us
  blocking collectives: 47.3 us -> 18.3 us
  starting transfers between devices: 22.4 us -> 40 us
  local copies, waits for them, and re-layouts: 20.1 us -> 27 us
    all_gather x1, waiting for transfers between devices: 12.6 us -> 112 us  [body(): lax.all_gather(right_vals[None], 'row', axis=0, tiled=True)]
    all_to_all x0 -> x2, waiting for transfers between devices: none -> 55.7 us  [the longest x1 39.1 us: gather_over(): return jnp.concatenate(lax.all_to_all(repeated, axis, 0, 0), axis=along)]
    all_gather x1 -> x0, waiting for transfers between devices: 55 us -> none  [body(): lax.all_gather(left_vals[None], 'col', axis=0, tiled=True)]
    all_to_all x1 -> x0, blocking collectives: 25.3 us -> none  [body(): lax.all_to_all(left_vals, 'depth', split_axis=0, concat_axis=0, tiled=True)]
    all_to_all x0 -> x2, starting transfers between devices: none -> 12 us  [the longest x1 8.47 us: gather_over(): return jnp.concatenate(lax.all_to_all(repeated, axis, 0, 0), axis=along)]
    reduce_scatter x1, waiting for transfers between devices: 47.2 us -> 55 us  [body(): lax.psum_scatter(partial_sum[None, None], 'depth', scatter_dimension=2, t...]
    another operation x0 -> x1, local copies, waits for them, and re-layouts: none -> 5.33 us  [gather_over(): repeated = jnp.stack([x] * lax.axis_size(axis))]
    all_to_all x1, starting transfers between devices: 3.28 us -> 6.93 us  [body(): lax.all_to_all(left_cols, 'depth', split_axis=0, concat_axis=0, tiled=True)]
  transfers between devices with their start and end apart: 7 -> 8, of which waited for: 7 -> 8; matrix products, arithmetic and copies ran while one was open for 5% -> 4% of each run, Pallas kernels for 0% -> 0%
where the time goes in v1:
time: 349 us
  waiting for transfers between devices  241 us (69%)
  starting transfers between devices  40 us (11%)
  local copies, waits for them, and re-layouts  27 us (8%)
  blocking collectives  18.3 us (5%)
  between operations  14.3 us (4%)
  other arithmetic  4 us (1%)
  matrix products  3.76 us (1%)
    all_gather x1, waiting for transfers between devices, body(): lax.all_gather(right_vals[None], 'row', axis=0, tiled=True)  112 us
    reduce_scatter x1, waiting for transfers between devices, body(): lax.psum_scatter(partial_sum[None, None], 'depth', scatter_dimension=2, t...  55 us
    all_to_all x1, waiting for transfers between devices, gather_over(): return jnp.concatenate(lax.all_to_all(repeated, axis, 0, 0), axis=along)  39.1 us
    all_to_all x1, blocking collectives, body(): lax.all_to_all(right_vals, 'col', split_axis=0, concat_axis=0, tiled=True)  18.3 us
    all_to_all x1, waiting for transfers between devices, body(): lax.all_to_all(left_vals, 'depth', split_axis=0, concat_axis=0, tiled=True)  16.6 us
    all_to_all x2, starting transfers between devices, gather_by_exchange(): return lax.all_to_all(copies, axis, split_axis=0, concat_axis=0, tiled=True)  11.9 us
    all_to_all x1, starting transfers between devices, body(): lax.all_to_all(right_cols, 'col', split_axis=0, concat_axis=0, tiled=True)  9.16 us
    all_to_all x1, starting transfers between devices, gather_over(): return jnp.concatenate(lax.all_to_all(repeated, axis, 0, 0), axis=along)  8.47 us
  transfers between devices with their start and end apart: 8, of which 8 were waited for; matrix products, arithmetic and copies ran while one was open for 4% of the time, Pallas kernels for 0%

profile of v1, /device:TPU:4, one launch (start us, length us, event | category | flops | bytes accessed | tf_op | source)
XLA Modules:
  0.0 348.5 jit_solution(2259339694360486009)
XLA Ops:
  7.2 0.7 and_select_fusion.7
  8.5 0.7 fusion.30
  9.2 0.8 scatter_custom_fusion.2
  9.9 0.7 reshape.1074
  10.6 9.2 %all-to-all-start.4 = ((s32[16,1,2]{2,1,0:T(1,128)}), s32[16,1,2]{2,1,0:T(1,128)S(1)}, u32[]{:S(2)}, u32[]{:S(2)}) async-start(s32[16,1,2]{2,1,0:T(1,128)} %bitcast.16), calls=%async_computation.4 | async-start | bytes 16384 | tf_op jit(solution)/shard_map/all_to_all | solution.py:85
  19.8 0.8 scatter_custom_fusion.1
  20.5 0.7 reshape.1072
  21.2 2.4 all-to-all-done.4
  23.5 6.9 %all-to-all-start.2 = ((s32[8,1,2]{2,1,0:T(1,128)}), s32[8,1,2]{2,1,0:T(1,128)S(1)}, u32[]{:S(2)}, u32[]{:S(2)}) async-start(s32[8,1,2]{2,1,0:T(1,128)} %bitcast.12), calls=%async_computation.2 | async-start | bytes 8192 | tf_op jit(solution)/shard_map/all_to_all | solution.py:65
  30.6 7.6 %all-to-all-done.2 = s32[8,1,2]{2,1,0:T(1,128)S(1)} async-done(((s32[8,1,2]{2,1,0:T(1,128)}), s32[8,1,2]{2,1,0:T(1,128)S(1)}, u32[]{:S(2)}, u32[]{:S(2)}) %all-to-all-start.2) | async-done | bytes 96 | tf_op jit(solution)/shard_map/all_to_all | solution.py:65
  38.7 6.2 %all-to-all-start.5 = ((s32[4,16,1,2]{1,3,2,0:T(2,128)}), s32[4,16,1,2]{1,3,2,0:T(2,128)S(1)}, u32[]{:S(2)}, u32[]{:S(2)}) async-start(s32[4,16,1,2]{1,3,2,0:T(2,128)} %broadcast_in_dim.126), calls=%async_computation.5 | async-start | bytes 8192 | tf_op jit(solution)/shard_map/all_to_all | solution.py:38
  45.0 7.6 %all-to-all-done.5 = s32[4,16,1,2]{1,3,2,0:T(2,128)S(1)} async-done(((s32[4,16,1,2]{1,3,2,0:T(2,128)}), s32[4,16,1,2]{1,3,2,0:T(2,128)S(1)}, u32[]{:S(2)}, u32[]{:S(2)}) %all-to-all-start.5) | async-done | bytes 544 | tf_op jit(solution)/shard_map/all_to_all | solution.py:38
  52.6 0.6 broadcast_in_dim.121
  53.2 5.7 %all-to-all-start.3 = ((s32[16,8,1,2]{1,3,2,0:T(2,128)}), s32[16,8,1,2]{1,3,2,0:T(2,128)S(1)}, u32[]{:S(2)}, u32[]{:S(2)}) async-start(s32[16,8,1,2]{1,3,2,0:T(2,128)} %broadcast_in_dim.121), calls=%async_computation.3 | async-start | bytes 32768 | tf_op jit(solution)/shard_map/all_to_all | solution.py:38
  58.9 0.9 broadcast_in_dim.117
  59.8 2.9 scatter_fusion
  62.8 3.5 %all-to-all-start = ((bf16[8,1,2,128,128]{4,3,2,1,0:T(8,128)(2,1)}), bf16[8,1,2,128,128]{4,3,2,1,0:T(8,128)(2,1)S(1)}, u32[]{:S(2)}, u32[]{:S(2)}) async-start(bf16[8,1,2,128,128]{4,3,2,1,0:T(8,128)(2,1)} %bitcast.7), calls=%async_computation | async-start | bytes 1048576 | tf_op jit(solution)/shard_map/all_to_all | solution.py:64
  66.5 1.1 scatter_fusion.1
  67.7 16.6 %all-to-all-done = bf16[8,1,2,128,128]{4,3,2,1,0:T(8,128)(2,1)S(1)} async-done(((bf16[8,1,2,128,128]{4,3,2,1,0:T(8,128)(2,1)}), bf16[8,1,2,128,128]{4,3,2,1,0:T(8,128)(2,1)S(1)}, u32[]{:S(2)}, u32[]{:S(2)}) %all-to-all-start) | async-done | bytes 524320 | tf_op jit(solution)/shard_map/all_to_all | solution.py:64
  84.3 18.3 %all_to_all.38 = bf16[16,1,2,128,128]{4,3,2,1,0:T(8,128)(2,1)} all-to-all(bf16[16,1,2,128,128]{4,3,2,1,0:T(8,128)(2,1)S(1)} %bitcast.93), channel_id=1, replica_groups=mesh['row'=4,'col'=16,'depth'=8] {'col'}, dimensions={0} | all-to-all | bytes 2097152 | tf_op jit(solution)/shard_map/all_to_all | solution.py:84
  102.6 5.3 %stack.3 = bf16[16,1,8,1,2,128,128]{6,5,4,3,2,1,0:T(8,128)(2,1)} broadcast(bf16[8,2,128,128]{3,2,1,0:T(8,128)(2,1)S(1)} %bitcast.95), dimensions={2,4,5,6} | broadcast | bytes 8912896 | tf_op jit(solution)/shard_map/stack | solution.py:9
  108.0 8.5 %all-to-all-start.1 = ((bf16[16,1,8,1,2,128,128]{6,5,4,3,2,1,0:T(8,128)(2,1)}), bf16[16,1,8,1,2,128,128]{6,5,4,3,2,1,0:T(8,128)(2,1)}, u32[]{:S(2)}, u32[]{:S(2)}) async-start(bf16[16,1,8,1,2,128,128]{6,5,4,3,2,1,0:T(8,128)(2,1)} %stack.3), calls=%async_computation.1 | async-start | bytes 16777216 | tf_op jit(solution)/shard_map/all_to_all | solution.py:10
  116.5 0.7 all-gather.3.cloned.1.call-update
  118.3 0.8 gather_fusion.1
  119.5 0.6 gather_fusion.2
  121.3 112.1 %all-gather.3.cloned.1.call-done = bf16[64,1,2,128,128]{4,3,2,1,0:T(8,128)(2,1)} async-done(((bf16[16,1,2,128,128]{4,3,2,1,0:T(8,128)(2,1)}), bf16[64,1,2,128,128]{4,3,2,1,0:T(8,128)(2,1)}) %all-gather.3.cloned.1.call-update) | async-done | bytes 4194320 | tf_op jit(solution)/shard_map/all_gather | solution.py:88
  233.4 3.1 gather_fusion.3
  236.6 39.1 %all-to-all-done.1 = bf16[16,1,8,1,2,128,128]{6,5,4,3,2,1,0:T(8,128)(2,1)} async-done(((bf16[16,1,8,1,2,128,128]{6,5,4,3,2,1,0:T(8,128)(2,1)}), bf16[16,1,8,1,2,128,128]{6,5,4,3,2,1,0:T(8,128)(2,1)}, u32[]{:S(2)}, u32[]{:S(2)}) %all-to-all-start.1) | async-done | bytes 8388640 | tf_op jit(solution)/shard_map/all_to_all | solution.py:10
  275.6 5.6 %gather_fusion = bf16[64,128,128]{2,1,0:T(8,128)(2,1)} fusion(bf16[256,128,128]{2,1,0:T(8,128)(2,1)} %bitcast.9, s32[1024]{0:T(1024)S(1)} %pad_clamp_fusion.3), kind=kCustom, calls=%fused_computation | custom fusion | bytes 4194560 | tf_op jit(solution)/shard_map/jit(_take)/gather | solution.py:100
  281.2 3.8 %fusion.7 = f32[1,1,32,128,128]{4,3,2,1,0:T(8,128)} fusion(bf16[32,2,128,128]{3,2,1,0:T(8,128)(2,1)S(1)} %bitcast.96, pred[32,2]{1,0:T(8,128)(4,1)S(1)} %copy.52, pred[32,2]{1,0:T(8,128)(4,1)S(1)} %get-tuple-element.5, bf16[32,2,128,128]{3,2,1,0:T(8,128)(2,1)} %bitcast.97, pred[32,2]{1,0:T(8,128)(4,1)S(1)} %copy.38), kind=kOutput, calls=%fused_computation.15 | convolution fusion | flops 271581184 | bytes 6291648 | tf_op jit(solution)/shard_map/pqab,pqbc->pac/dot_general | solution.py:117
  285.0 55.0 %reduce-scatter.2.cloned.1.call-done = f32[1,1,4,128,128]{4,3,2,1,0:T(8,128)} async-done(((f32[1,1,32,128,128]{4,3,2,1,0:T(8,128)}), f32[1,1,4,128,128]{4,3,2,1,0:T(8,128)}) %reduce-scatter.2.cloned.1.call-update) | async-done | bytes 262160 | tf_op jit(solution)/shard_map/reduce_scatter | solution.py:120
  340.0 1.7 log-plus-one_convert_fusion
  (53 shorter events, 4.3 us)
Async XLA Ops:
  10.6 12.9 %all-to-all-start.4 = ((s32[16,1,2]{2,1,0:T(1,128)}), s32[16,1,2]{2,1,0:T(1,128)S(1)}, u32[]{:S(2)}, u32[]{:S(2)}) async-start(s32[16,1,2]{2,1,0:T(1,128)} %bitcast.16), calls=%async_computation.4 | async-start | bytes 16384 | tf_op jit(solution)/shard_map/all_to_all | solution.py:85
  23.5 14.6 %all-to-all-start.2 = ((s32[8,1,2]{2,1,0:T(1,128)}), s32[8,1,2]{2,1,0:T(1,128)S(1)}, u32[]{:S(2)}, u32[]{:S(2)}) async-start(s32[8,1,2]{2,1,0:T(1,128)} %bitcast.12), calls=%async_computation.2 | async-start | bytes 8192 | tf_op jit(solution)/shard_map/all_to_all | solution.py:65
  38.7 13.9 %all-to-all-start.5 = ((s32[4,16,1,2]{1,3,2,0:T(2,128)}), s32[4,16,1,2]{1,3,2,0:T(2,128)S(1)}, u32[]{:S(2)}, u32[]{:S(2)}) async-start(s32[4,16,1,2]{1,3,2,0:T(2,128)} %broadcast_in_dim.126), calls=%async_computation.5 | async-start | bytes 8192 | tf_op jit(solution)/shard_map/all_to_all | solution.py:38
  53.2 9.6 %all-to-all-start.3 = ((s32[16,8,1,2]{1,3,2,0:T(2,128)}), s32[16,8,1,2]{1,3,2,0:T(2,128)S(1)}, u32[]{:S(2)}, u32[]{:S(2)}) async-start(s32[16,8,1,2]{1,3,2,0:T(2,128)} %broadcast_in_dim.121), calls=%async_computation.3 | async-start | bytes 32768 | tf_op jit(solution)/shard_map/all_to_all | solution.py:38
  58.9 7.6 %copy-start = (bf16[1,1,16,128,128]{4,3,2,1,0:T(8,128)(2,1)S(1)}, bf16[1,1,16,128,128]{4,3,2,1,0:T(8,128)(2,1)}, u32[]{:S(2)}) copy-start(bf16[1,1,16,128,128]{4,3,2,1,0:T(8,128)(2,1)} %param.4) | copy-start | bytes 1572868
  62.8 21.5 %all-to-all-start = ((bf16[8,1,2,128,128]{4,3,2,1,0:T(8,128)(2,1)}), bf16[8,1,2,128,128]{4,3,2,1,0:T(8,128)(2,1)S(1)}, u32[]{:S(2)}, u32[]{:S(2)}) async-start(bf16[8,1,2,128,128]{4,3,2,1,0:T(8,128)(2,1)} %bitcast.7), calls=%async_computation | async-start | bytes 1048576 | tf_op jit(solution)/shard_map/all_to_all | solution.py:64
  108.0 9.3 %copy-start.1 = (s32[1,1,32,2]{2,3,1,0:T(2,128)S(1)}, s32[1,1,32,2]{2,3,1,0:T(2,128)}, u32[]{:S(2)}) copy-start(s32[1,1,32,2]{2,3,1,0:T(2,128)} %param.7) | copy-start | bytes 772
  108.0 167.6 %all-to-all-start.1 = ((bf16[16,1,8,1,2,128,128]{6,5,4,3,2,1,0:T(8,128)(2,1)}), bf16[16,1,8,1,2,128,128]{6,5,4,3,2,1,0:T(8,128)(2,1)}, u32[]{:S(2)}, u32[]{:S(2)}) async-start(bf16[16,1,8,1,2,128,128]{6,5,4,3,2,1,0:T(8,128)(2,1)} %stack.3), calls=%async_computation.1 | async-start | bytes 16777216 | tf_op jit(solution)/shard_map/all_to_all | solution.py:10
  116.5 117.0 %all-gather.3.cloned.1.call-start = ((), (), s32[]{:S(2)}) async-start(), calls=%async_computation.9 | async-start | bytes 5242880 | tf_op jit(solution)/shard_map/all_gather | solution.py:88
  117.2 222.8 %reduce-scatter.2.cloned.1.call-start = ((), (), s32[]{:S(2)}) async-start(), calls=%async_computation.8 | async-start | bytes 2359296 | tf_op jit(solution)/shard_map/reduce_scatter | solution.py:120
Sparse Core Ops, SparseCore 0:
  119.4 113.9 all-gather.2
  285.1 54.8 reduce-scatter.1
